TPU v7x, 512 devices: a whole 4x8x8 slice. The times are simulated.
512 devices in a mesh: section: 8 (over y), expert: 32 (over z, x_hi, core), dp: 2 (over x_lo).
Axes of the slice: x: 4 (x_hi: 2, x_lo: 2; x = x_hi * 2 + x_lo), y: 8, z: 8, core: 2. Of those that a mesh axis runs over, the one named last changes fastest.
Arguments:
- blocks: bfloat16 [8, 512, 7168], P('section', ('expert', 'dp')), may hold values from -6 to 6
- gains: float32 [8, 7168], P('section'), may hold values from 0.1 to 1.9
- w_gate: bfloat16 [8, 7168, 4096], P('section', 'dp', 'expert'), may hold values from -0.0625 to 0.0625
- w_up: bfloat16 [8, 7168, 4096], P('section', 'dp', 'expert'), may hold values from -0.0625 to 0.0625
- w_down: bfloat16 [8, 7168, 4096], P('section', 'dp', 'expert'), may hold values from -0.1875 to 0.1875
- expert_ids: int32 [8, 2, 512, 2], P('section', None, ('expert', 'dp')), may hold values from 0 to 3, all different within a row; in each aligned block of 8 rows (0 to 7, 8 to 15, ..., all dimensions but the last counted through in order) at most 5 rows name the same one
- combine: float32 [8, 2, 512, 2], P('section', None, ('expert', 'dp')), may hold values from 0.2 to 1
Outputs:
- finished: bfloat16 [8, 512, 7168], P('section', ('expert', 'dp'))
Inputs may be any that keep to these rules, and one draw needn't show every extreme that they name: `expert_ids`: each token names 2 different experts; within the 8 tokens of one device (aligned blocks), no expert is named more than 5 times, a bound that some block reaches.
All inputs are finite; a program needn't handle non-finite values.
Results may differ from a plain program's by a relative error of at most 0.0073.
Values may be sent and summed in bfloat16 or wider, within the bound.
No kernel may reach another device: no remote copies, remote signals or barrier semaphores. Data moves between devices by JAX's collectives and lax.ppermute only.
A program may use at most 64 MiB of HBM per device.

v0:
```python
from functools import partial
import jax
import jax.numpy as jnp
import numpy as np
from jax import lax
from jax.sharding import Mesh
from jax.sharding import PartitionSpec as P

ALL = ("eg", "q", "dp")


def passed_along(array, axis, by):
    length = lax.axis_size(axis)
    return lax.ppermute(array, axis, [(i, (i + by) % length) for i in range(length)])


def route(stream, gain_row, routes, experts, capacity):
    tok_rows, model_width = stream.shape
    fan_out = routes.shape[1]
    widened = stream.astype(jnp.float32)
    inv_rms = lax.rsqrt(jnp.mean(widened * widened, axis=1, keepdims=True) + 1e-06)
    normed = (widened * inv_rms * gain_row[None, :]).astype(jnp.bfloat16)
    flat_ids = routes.reshape(-1)
    count_all = flat_ids.shape[0]
    chosen = (flat_ids[:, None] == jnp.arange(experts, dtype=jnp.int32)[None, :]).astype(
        jnp.float32
    )
    triangle = (jnp.arange(count_all)[:, None] >= jnp.arange(count_all)[None, :]).astype(
        jnp.float32
    )
    running = jnp.dot(triangle, chosen, preferred_element_type=jnp.float32)
    slot_of = jnp.sum(chosen * (running - 1.0), axis=1).astype(jnp.int32)
    target = flat_ids * capacity + slot_of
    placing = jnp.arange(experts * capacity, dtype=jnp.int32)[:, None] == target[None, :]
    placing = (
        placing.reshape(experts * capacity, tok_rows, fan_out).any(axis=2).astype(jnp.bfloat16)
    )
    outgoing = jnp.dot(placing, normed, preferred_element_type=jnp.float32).astype(jnp.bfloat16)
    return (widened, outgoing.reshape(experts, capacity, model_width), target)


def moe_layer(stream, gain_row, gate_w, up_w, down_mine, routes, mixing):
    experts = lax.axis_size("eg")
    blocks = lax.axis_size("q")
    halves = lax.axis_size("dp")
    tok_rows, model_width = stream.shape
    fan_out = routes.shape[1]
    capacity = min(tok_rows, max(2, 5 * tok_rows * fan_out // (4 * experts)))
    half = model_width // halves
    widened, outgoing, target = route(stream, gain_row, routes, experts, capacity)
    lanes = 128
    tiles = half // lanes
    send = outgoing.reshape(experts, capacity, halves, tiles, lanes).transpose(0, 2, 1, 3, 4)
    send = send.reshape(experts * halves, 2, capacity * half // 2)
    arrived = lax.all_to_all(send, ("eg", "dp"), split_axis=0, concat_axis=0, tiled=True)
    arrived = arrived.reshape(experts * halves, capacity, half).transpose(1, 0, 2)
    arrived = lax.all_gather(arrived, "q", axis=1, tiled=True)
    sources = blocks * experts * halves
    rows = arrived.reshape(capacity * sources, half)
    units = gate_w.shape[1]
    both_w = jnp.concatenate([gate_w, up_w], axis=1)
    gate_up = jnp.dot(rows, both_w, preferred_element_type=jnp.float32)
    mine = gate_up.reshape(rows.shape[0], 2, units).transpose(1, 0, 2)
    both = mine + passed_along(mine.astype(jnp.bfloat16), "dp", 1).astype(jnp.float32)
    hidden = (jax.nn.silu(both[0]) * both[1]).astype(jnp.bfloat16)
    hidden_all = lax.all_gather(hidden, "q", axis=1, tiled=True)
    out = lax.dot_general(
        hidden_all, down_mine, (((1,), (1,)), ((), ())), preferred_element_type=jnp.float32
    ).astype(jnp.bfloat16)
    piece = out.shape[1]
    out = out.reshape(capacity, blocks, experts, halves, piece).transpose(2, 1, 3, 0, 4)
    back = lax.all_to_all(
        out.reshape(sources, 2, capacity * piece // 2), ALL, split_axis=0, concat_axis=0, tiled=True
    )
    back = back.reshape(experts, blocks, halves, capacity, piece).transpose(0, 3, 2, 1, 4)
    expert_out = back.reshape(experts * capacity, model_width)
    picked = jnp.take(expert_out, target, axis=0)
    picked = picked.reshape(tok_rows, fan_out, model_width)
    mixed_sum = jnp.sum(mixing[:, :, None] * picked.astype(jnp.float32), axis=1)
    return (widened + mixed_sum).astype(jnp.bfloat16)


def on_device(blocks, gains, w_gate, w_up, w_down, expert_ids, combine):
    stream = blocks[0]
    turns = expert_ids.shape[1]
    n_blocks = lax.axis_size("q")
    down_local = w_down[0]
    half, width = down_local.shape
    piece = half // n_blocks
    down_mine = lax.all_to_all(
        down_local.reshape(n_blocks, piece, width), "q", split_axis=0, concat_axis=0, tiled=True
    )
    down_mine = down_mine.transpose(1, 0, 2).reshape(piece, n_blocks * width)
    for layer_turn in range(turns):
        if layer_turn > 0:
            stream = passed_along(stream, "section", 1)
        stream = moe_layer(
            stream,
            gains[0],
            w_gate[0],
            w_up[0],
            down_mine,
            expert_ids[0, layer_turn],
            combine[0, layer_turn],
        )
    return stream[None]


def solution(mesh):
    n_section, n_expert, n_dp = (mesh.shape[a] for a in ("section", "expert", "dp"))
    n_q = n_expert // 4
    inner = Mesh(
        np.asarray(mesh.devices).reshape(n_section, n_expert // n_q, n_q, n_dp),
        ("section", "eg", "q", "dp"),
    )
    tok = ("eg", "q", "dp")
    in_specs = (
        P("section", tok, None),
        P("section", None),
        P("section", "dp", ("eg", "q")),
        P("section", "dp", ("eg", "q")),
        P("section", "dp", ("eg", "q")),
        P("section", None, tok, None),
        P("section", None, tok, None),
    )
    out_specs = P("section", tok, None)
    return jax.shard_map(
        on_device, mesh=inner, in_specs=in_specs, out_specs=out_specs, check_vma=False
    )
```

profile of v0, /device:TPU:1, one launch (start us, length us, event | category | flops | bytes accessed | tf_op | source)
XLA Modules:
  0.0 239.1 jit_solution(17253363982797982586)
XLA Ops:
  6.5 0.7 fusion.32
  8.2 0.7 bitcast_add_fusion.1
  9.0 1.1 fusion.12
  10.1 1.2 convolution_convert_fusion.1
  11.7 21.9 %all_to_all.25 = bf16[8,2,8960]{2,1,0:T(2,128)(2,1)S(1)} all-to-all(bf16[8,2,8960]{2,1,0:T(2,128)(2,1)S(1)} %reshape.126), channel_id=1, replica_groups=mesh['section'=8,'eg'=4,'q'=8,'dp'=2] {'eg','dp'}, dimensions={0} | all-to-all | bytes 573440 | tf_op jit(solution)/shard_map/all_to_all | solution.py:55
  33.8 0.8 copy.57
  34.6 8.1 %all-to-all-start.1 = ((bf16[8,448,128]{2,1,0:T(8,128)(2,1)}), bf16[8,448,128]{2,1,0:T(8,128)(2,1)}, u32[]{:S(2)}, u32[]{:S(2)}) async-start(bf16[8,448,128]{2,1,0:T(8,128)(2,1)} %bitcast.16), calls=%async_computation.1 | async-start | bytes 1835008 | tf_op jit(solution)/shard_map/all_to_all | solution.py:90
  42.7 1.4 maximum_bitcast_fusion
  44.1 2.7 %copy.58 = bf16[256,3584]{1,0:T(8,128)(2,1)} copy(bf16[256,3584]{0,1:T(8,128)(2,1)S(1)} %maximum_bitcast_fusion) | data formatting | bytes 3670016 | tf_op jit(solution)/shard_map/dot_general | solution.py:62
  46.8 21.7 %all-gather.3.cloned.1.call-done = bf16[5,64,3584]{2,1,0:T(8,128)(2,1)} async-done(((bf16[5,8,3584]{2,1,0:T(8,128)(2,1)}), bf16[5,64,3584]{2,1,0:T(8,128)(2,1)}) %all-gather.3.cloned.1.call-update) | async-done | bytes 2293776 | tf_op jit(solution)/shard_map/all_gather | solution.py:57
  68.5 3.0 %fusion.33 = (bf16[2,320,128]{2,1,0:T(8,128)(2,1)S(1)}, f32[2,320,128]{2,1,0:T(8,128)S(1)}) fusion(bf16[320,3584,1]{1,0,2:T(8,128)(2,1)} %bitcast.110, bf16[2,128,3584]{2,1,0:T(8,128)(2,1)} %bitcast.100), kind=kOutput, calls=%fused_computation.77 | convolution fusion | flops 587284480 | bytes 4620288 | tf_op jit(solution)/shard_map/dot_general | solution.py:62
  71.5 2.3 collective-permute-start
  73.8 5.1 %collective-permute-done = bf16[2,320,128]{2,1,0:T(8,128)(2,1)S(1)} collective-permute-done((bf16[2,320,128]{2,1,0:T(8,128)(2,1)S(1)}, bf16[2,320,128]{2,1,0:T(8,128)(2,1)S(1)}, u32[]{:S(2)}, u32[]{:S(2)}) %collective-permute-start) | collective-permute-done | bytes 163872 | tf_op jit(solution)/shard_map/ppermute | solution.py:14
  79.0 17.6 %all_gather.13 = bf16[320,1024]{1,0:T(8,128)(2,1)S(1)} all-gather(bf16[320,128]{1,0:T(8,128)(2,1)S(1)} %fusion.19), channel_id=1, replica_groups=mesh['section'=8,'eg'=4,'q'=8,'dp'=2] {'q'}, dimensions={1}, use_global_device_ids=true | all-gather | bytes 737280 | tf_op jit(solution)/shard_map/all_gather | solution.py:66
  96.6 1.7 convolution_convert_fusion.3
  98.7 1.4 reshape.131
  100.1 6.1 %all-to-all-start.2 = ((bf16[64,2,1120]{2,1,0:T(2,128)(2,1)}), bf16[64,2,1120]{2,1,0:T(2,128)(2,1)S(1)}, u32[]{:S(2)}, u32[]{:S(2)}) async-start(bf16[64,2,1120]{2,1,0:T(2,128)(2,1)} %reshape.131), calls=%async_computation.2 | async-start | bytes 589824 | tf_op jit(solution)/shard_map/all_to_all | solution.py:72
  106.4 13.8 %all-to-all-done.2 = bf16[64,2,1120]{2,1,0:T(2,128)(2,1)S(1)} async-done(((bf16[64,2,1120]{2,1,0:T(2,128)(2,1)}), bf16[64,2,1120]{2,1,0:T(2,128)(2,1)S(1)}, u32[]{:S(2)}, u32[]{:S(2)}) %all-to-all-start.2) | async-done | bytes 286752 | tf_op jit(solution)/shard_map/all_to_all | solution.py:72
  123.1 3.1 %collective-permute-start.1 = (bf16[8,7168]{1,0:T(8,128)(2,1)S(1)}, bf16[8,7168]{1,0:T(8,128)(2,1)S(1)}, u32[]{:S(2)}, u32[]{:S(2)}) collective-permute-start(bf16[8,7168]{1,0:T(8,128)(2,1)S(1)} %fusion.15), channel_id=1, source_target_pairs={{0,64},{64,128},{128,192},{192,256},{256,320},{320,384},{384,448},... | collective-permute-start | bytes 344072 | tf_op jit(solution)/shard_map/ppermute | solution.py:14
  126.3 4.7 %collective-permute-done.1 = bf16[8,7168]{1,0:T(8,128)(2,1)S(1)} collective-permute-done((bf16[8,7168]{1,0:T(8,128)(2,1)S(1)}, bf16[8,7168]{1,0:T(8,128)(2,1)S(1)}, u32[]{:S(2)}, u32[]{:S(2)}) %collective-permute-start.1) | collective-permute-done | bytes 114720 | tf_op jit(solution)/shard_map/ppermute | solution.py:14
  131.9 12.6 %all_to_all.26 = bf16[8,2,8960]{2,1,0:T(2,128)(2,1)S(1)} all-to-all(bf16[8,2,8960]{2,1,0:T(2,128)(2,1)S(1)} %reshape.134), channel_id=1, replica_groups=mesh['section'=8,'eg'=4,'q'=8,'dp'=2] {'eg','dp'}, dimensions={0} | all-to-all | bytes 573440 | tf_op jit(solution)/shard_map/all_to_all | solution.py:55
  144.7 0.8 copy.66
  145.5 30.4 %all-gather.5.cloned.1.call-done = bf16[5,64,3584]{2,1,0:T(8,128)(2,1)} async-done(((bf16[5,8,3584]{2,1,0:T(8,128)(2,1)}), bf16[5,64,3584]{2,1,0:T(8,128)(2,1)}) %all-gather.5.cloned.1.call-update) | async-done | bytes 2293776 | tf_op jit(solution)/shard_map/all_gather | solution.py:57
  175.9 2.4 %fusion.34 = (bf16[2,320,128]{2,1,0:T(8,128)(2,1)S(1)}, f32[2,320,128]{2,1,0:T(8,128)S(1)}) fusion(bf16[320,3584,1]{1,0,2:T(8,128)(2,1)} %bitcast.111, bf16[2,128,3584]{2,1,0:T(8,128)(2,1)S(1)} %bitcast.101), kind=kOutput, calls=%fused_computation.78 | convolution fusion | flops 587284480 | bytes 4620288 | tf_op jit(solution)/shard_map/dot_general | solution.py:62
  178.3 2.2 collective-permute-start.2
  180.5 5.2 %collective-permute-done.2 = bf16[2,320,128]{2,1,0:T(8,128)(2,1)S(1)} collective-permute-done((bf16[2,320,128]{2,1,0:T(8,128)(2,1)S(1)}, bf16[2,320,128]{2,1,0:T(8,128)(2,1)S(1)}, u32[]{:S(2)}, u32[]{:S(2)}) %collective-permute-start.2) | collective-permute-done | bytes 163872 | tf_op jit(solution)/shard_map/ppermute | solution.py:14
  185.8 17.7 %all_gather.15 = bf16[320,1024]{1,0:T(8,128)(2,1)S(1)} all-gather(bf16[320,128]{1,0:T(8,128)(2,1)S(1)} %fusion.17), channel_id=1, replica_groups=mesh['section'=8,'eg'=4,'q'=8,'dp'=2] {'q'}, dimensions={1}, use_global_device_ids=true | all-gather | bytes 737280 | tf_op jit(solution)/shard_map/all_gather | solution.py:66
  203.5 1.7 convolution_convert_fusion.2
  205.6 1.4 reshape.138
  207.0 7.8 %all-to-all-start.4 = ((bf16[64,2,1120]{2,1,0:T(2,128)(2,1)}), bf16[64,2,1120]{2,1,0:T(2,128)(2,1)S(1)}, u32[]{:S(2)}, u32[]{:S(2)}) async-start(bf16[64,2,1120]{2,1,0:T(2,128)(2,1)} %reshape.138), calls=%async_computation.4 | async-start | bytes 589824 | tf_op jit(solution)/shard_map/all_to_all | solution.py:72
  214.8 13.8 %all-to-all-done.4 = bf16[64,2,1120]{2,1,0:T(2,128)(2,1)S(1)} async-done(((bf16[64,2,1120]{2,1,0:T(2,128)(2,1)}), bf16[64,2,1120]{2,1,0:T(2,128)(2,1)S(1)}, u32[]{:S(2)}, u32[]{:S(2)}) %all-to-all-start.4) | async-done | bytes 286752 | tf_op jit(solution)/shard_map/all_to_all | solution.py:72
  229.9 0.7 gather_fusion.1
  (71 shorter events, 9.7 us)
Async XLA Ops:
  6.5 62.0 %all-gather.3.cloned.1.call-start = ((), (), s32[]{:S(2)}) async-start(), calls=%async_computation.5 | async-start | bytes 2580480 | tf_op jit(solution)/shard_map/all_gather | solution.py:57
  11.6 31.2 %copy-start.2 = (bf16[1,3584,128]{2,1,0:T(8,128)(2,1)S(1)}, bf16[1,3584,128]{2,1,0:T(8,128)(2,1)}, u32[]{:S(2)}) copy-start(bf16[1,3584,128]{2,1,0:T(8,128)(2,1)} %param.12) | copy-start | bytes 2752516
  34.6 62.0 %all-to-all-start.1 = ((bf16[8,448,128]{2,1,0:T(8,128)(2,1)}), bf16[8,448,128]{2,1,0:T(8,128)(2,1)}, u32[]{:S(2)}, u32[]{:S(2)}) async-start(bf16[8,448,128]{2,1,0:T(8,128)(2,1)} %bitcast.16), calls=%async_computation.1 | async-start | bytes 1835008 | tf_op jit(solution)/shard_map/all_to_all | solution.py:90
  71.5 7.4 %collective-permute-start = (bf16[2,320,128]{2,1,0:T(8,128)(2,1)S(1)}, bf16[2,320,128]{2,1,0:T(8,128)(2,1)S(1)}, u32[]{:S(2)}, u32[]{:S(2)}) collective-permute-start(bf16[2,320,128]{2,1,0:T(8,128)(2,1)S(1)} %get-tuple-element.16), channel_id=1, source_target_pairs={{0,1},{1,0},{2,3},{3,2},{4,5},{5,4},{6,7},{7,6},{8,9},{9,8},{10,11... | collective-permute-start | bytes 491528 | tf_op jit(solution)/shard_map/ppermute | solution.py:14
  96.6 9.6 %copy-start.4 = (f32[1,2,8,2]{2,3,1,0:T(2,128)S(1)}, f32[1,2,8,2]{2,3,1,0:T(2,128)}, u32[]{:S(2)}) copy-start(f32[1,2,8,2]{2,3,1,0:T(2,128)} %param.15) | copy-start | bytes 388
  100.1 20.1 %all-to-all-start.2 = ((bf16[64,2,1120]{2,1,0:T(2,128)(2,1)}), bf16[64,2,1120]{2,1,0:T(2,128)(2,1)S(1)}, u32[]{:S(2)}, u32[]{:S(2)}) async-start(bf16[64,2,1120]{2,1,0:T(2,128)(2,1)} %reshape.131), calls=%async_computation.2 | async-start | bytes 589824 | tf_op jit(solution)/shard_map/all_to_all | solution.py:72
  106.2 69.7 %all-gather.5.cloned.1.call-start = ((), (), s32[]{:S(2)}) async-start(), calls=%async_computation.6 | async-start | bytes 2580480 | tf_op jit(solution)/shard_map/all_gather | solution.py:57
  121.3 1.7 copy-start.1
  121.3 9.8 %copy-start.3 = (f32[1,7168]{1,0:T(1,128)S(1)}, f32[1,7168]{1,0:T(1,128)}, u32[]{:S(2)}) copy-start(f32[1,7168]{1,0:T(1,128)} %param.10) | copy-start | bytes 86020
  123.1 7.9 %collective-permute-start.1 = (bf16[8,7168]{1,0:T(8,128)(2,1)S(1)}, bf16[8,7168]{1,0:T(8,128)(2,1)S(1)}, u32[]{:S(2)}, u32[]{:S(2)}) collective-permute-start(bf16[8,7168]{1,0:T(8,128)(2,1)S(1)} %fusion.15), channel_id=1, source_target_pairs={{0,64},{64,128},{128,192},{192,256},{256,320},{320,384},{384,448},... | collective-permute-start | bytes 344072 | tf_op jit(solution)/shard_map/ppermute | solution.py:14
  131.2 44.7 %copy-start = (bf16[256,3584]{1,0:T(8,128)(2,1)S(1)}, bf16[256,3584]{1,0:T(8,128)(2,1)}, u32[]{:S(2)}) copy-start(bf16[256,3584]{1,0:T(8,128)(2,1)} %copy.58) | copy-start | bytes 5505028
  178.3 7.4 %collective-permute-start.2 = (bf16[2,320,128]{2,1,0:T(8,128)(2,1)S(1)}, bf16[2,320,128]{2,1,0:T(8,128)(2,1)S(1)}, u32[]{:S(2)}, u32[]{:S(2)}) collective-permute-start(bf16[2,320,128]{2,1,0:T(8,128)(2,1)S(1)} %get-tuple-element.18), channel_id=1, source_target_pairs={{0,1},{1,0},{2,3},{3,2},{4,5},{5,4},{6,7},{7,6},{8,9},{9,8},{10,11... | collective-permute-start | bytes 491528 | tf_op jit(solution)/shard_map/ppermute | solution.py:14
  207.0 21.7 %all-to-all-start.4 = ((bf16[64,2,1120]{2,1,0:T(2,128)(2,1)}), bf16[64,2,1120]{2,1,0:T(2,128)(2,1)S(1)}, u32[]{:S(2)}, u32[]{:S(2)}) async-start(bf16[64,2,1120]{2,1,0:T(2,128)(2,1)} %reshape.138), calls=%async_computation.4 | async-start | bytes 589824 | tf_op jit(solution)/shard_map/all_to_all | solution.py:72
Sparse Core Ops, SparseCore 0:
  34.8 33.7 all-gather.2
  145.6 30.2 all-gather.4
where the time goes:
time: 240 us; the launch traced here: 239 us
  waiting for transfers between devices  94.7 us (39%)
  blocking collectives  69.8 us (29%)
  starting transfers between devices  29.6 us (12%)
  local copies, waits for them, and re-layouts  14.7 us (6%)
  between operations  13.8 us (6%)
  matrix products  10.6 us (4%)
  other arithmetic  5.94 us (2%)
    all_gather x2, waiting for transfers between devices, moe_layer(): arrived = lax.all_gather(arrived, 'q', axis=1, tiled=True)  52.1 us
    all_gather x2, blocking collectives, moe_layer(): hidden_all = lax.all_gather(hidden, 'q', axis=1, tiled=True)  35.3 us
    all_to_all x2, blocking collectives, moe_layer(): lax.all_to_all(send, ('eg', 'dp'), split_axis=0, concat_axis=0, tiled=True)  34.5 us
    all_to_all x2, waiting for transfers between devices, moe_layer(): lax.all_to_all(out.reshape(sources, 2, capacity * piece // 2), ALL, split...  27.6 us
    ppermute x3, waiting for transfers between devices, passed_along(): lax.ppermute(array, axis, [(i, (i + by) % length) for i in range(length)])  14.9 us
    all_to_all x2, starting transfers between devices, moe_layer(): lax.all_to_all(out.reshape(sources, 2, capacity * piece // 2), ALL, split...  13.9 us
    all_to_all x1, starting transfers between devices, on_device(): lax.all_to_all(down_local.reshape(n_blocks, piece, width), 'q', split_axi...  8.1 us
    ppermute x3, starting transfers between devices, passed_along(): lax.ppermute(array, axis, [(i, (i + by) % length) for i in range(length)])  7.56 us
  transfers between devices with their start and end apart: 8, of which 7 were waited for; matrix products, arithmetic and copies ran while one was open for 3% of the time, Pallas kernels for 0%

commit v1 on v0

--- a/solution.py
+++ b/solution.py
@@ -63,7 +63,9 @@
     mine = gate_up.reshape(rows.shape[0], 2, units).transpose(1, 0, 2)
     both = mine + passed_along(mine.astype(jnp.bfloat16), "dp", 1).astype(jnp.float32)
     hidden = (jax.nn.silu(both[0]) * both[1]).astype(jnp.bfloat16)
-    hidden_all = lax.all_gather(hidden, "q", axis=1, tiled=True)
+    hidden_all = jnp.concatenate(
+        lax.all_to_all(jnp.stack([hidden] * lax.axis_size("q")), "q", 0, 0), axis=1
+    )
     out = lax.dot_general(
         hidden_all, down_mine, (((1,), (1,)), ((), ())), preferred_element_type=jnp.float32
     ).astype(jnp.bfloat16)

time: 240 us -> 239 us (level)
  blocking collectives: 69.8 us -> 67 us
    all_gather x2 -> x0, blocking collectives: 35.3 us -> none  [moe_layer(): hidden_all = lax.all_gather(hidden, 'q', axis=1, tiled=True)]
    all_to_all x0 -> x2, blocking collectives: none -> 32.5 us  [moe_layer(): lax.all_to_all(jnp.stack([hidden] * lax.axis_size('q')), 'q', 0, 0)]
where the time goes in v1:
time: 239 us; the launch traced here: 238 us
  waiting for transfers between devices  94.7 us (40%)
  blocking collectives  67 us (28%)
  starting transfers between devices  31.4 us (13%)
  local copies, waits for them, and re-layouts  14.9 us (6%)
  between operations  13.8 us (6%)
  matrix products  10.7 us (4%)
  other arithmetic  5.94 us (2%)
    all_gather x2, waiting for transfers between devices, moe_layer(): arrived = lax.all_gather(arrived, 'q', axis=1, tiled=True)  52.1 us
    all_to_all x2, blocking collectives, moe_layer(): lax.all_to_all(send, ('eg', 'dp'), split_axis=0, concat_axis=0, tiled=True)  34.5 us
    all_to_all x2, blocking collectives, moe_layer(): lax.all_to_all(jnp.stack([hidden] * lax.axis_size('q')), 'q', 0, 0)  32.5 us
    all_to_all x2, waiting for transfers between devices, moe_layer(): lax.all_to_all(out.reshape(sources, 2, capacity * piece // 2), ALL, split...  27.6 us
    all_to_all x2, starting transfers between devices, moe_layer(): lax.all_to_all(out.reshape(sources, 2, capacity * piece // 2), ALL, split...  15.7 us
    ppermute x3, waiting for transfers between devices, passed_along(): lax.ppermute(array, axis, [(i, (i + by) % length) for i in range(length)])  14.9 us
    all_to_all x1, starting transfers between devices, on_device(): lax.all_to_all(down_local.reshape(n_blocks, piece, width), 'q', split_axi...  8.1 us
    ppermute x3, starting transfers between devices, passed_along(): lax.ppermute(array, axis, [(i, (i + by) % length) for i in range(length)])  7.57 us
  transfers between devices with their start and end apart: 8, of which 7 were waited for; matrix products, arithmetic and copies ran while one was open for 3% of the time, Pallas kernels for 0%

profile of v1, /device:TPU:1, one launch (start us, length us, event | category | flops | bytes accessed | tf_op | source)
XLA Modules:
  0.0 238.3 jit_solution(16449250978074075804)
XLA Ops:
  6.5 0.7 fusion.34
  8.2 0.7 bitcast_add_fusion.1
  9.0 1.1 fusion.14
  10.1 1.2 convolution_convert_fusion.1
  11.7 21.9 %all_to_all.35 = bf16[8,2,8960]{2,1,0:T(2,128)(2,1)S(1)} all-to-all(bf16[8,2,8960]{2,1,0:T(2,128)(2,1)S(1)} %reshape.134), channel_id=1, replica_groups=mesh['section'=8,'eg'=4,'q'=8,'dp'=2] {'eg','dp'}, dimensions={0} | all-to-all | bytes 573440 | tf_op jit(solution)/shard_map/all_to_all | solution.py:55
  33.8 0.8 copy.55
  34.6 8.1 %all-to-all-start.2 = ((bf16[8,448,128]{2,1,0:T(8,128)(2,1)}), bf16[8,448,128]{2,1,0:T(8,128)(2,1)}, u32[]{:S(2)}, u32[]{:S(2)}) async-start(bf16[8,448,128]{2,1,0:T(8,128)(2,1)} %bitcast.16), calls=%async_computation.2 | async-start | bytes 1835008 | tf_op jit(solution)/shard_map/all_to_all | solution.py:92
  42.7 1.4 maximum_bitcast_fusion
  44.1 2.7 %copy.56 = bf16[256,3584]{1,0:T(8,128)(2,1)} copy(bf16[256,3584]{0,1:T(8,128)(2,1)S(1)} %maximum_bitcast_fusion) | data formatting | bytes 3670016 | tf_op jit(solution)/shard_map/dot_general | solution.py:62
  46.8 21.7 %all-gather.3.cloned.1.call-done = bf16[5,64,3584]{2,1,0:T(8,128)(2,1)} async-done(((bf16[5,8,3584]{2,1,0:T(8,128)(2,1)}), bf16[5,64,3584]{2,1,0:T(8,128)(2,1)}) %all-gather.3.cloned.1.call-update) | async-done | bytes 2293776 | tf_op jit(solution)/shard_map/all_gather | solution.py:57
  68.5 3.0 %fusion.35 = (bf16[2,320,128]{2,1,0:T(8,128)(2,1)S(1)}, f32[2,320,128]{2,1,0:T(8,128)S(1)}) fusion(bf16[320,3584,1]{1,0,2:T(8,128)(2,1)} %bitcast.98, bf16[2,128,3584]{2,1,0:T(8,128)(2,1)} %bitcast.88), kind=kOutput, calls=%fused_computation.77 | convolution fusion | flops 587284480 | bytes 4620288 | tf_op jit(solution)/shard_map/dot_general | solution.py:62
  71.5 2.3 collective-permute-start
  73.8 5.1 %collective-permute-done = bf16[2,320,128]{2,1,0:T(8,128)(2,1)S(1)} collective-permute-done((bf16[2,320,128]{2,1,0:T(8,128)(2,1)S(1)}, bf16[2,320,128]{2,1,0:T(8,128)(2,1)S(1)}, u32[]{:S(2)}, u32[]{:S(2)}) %collective-permute-start) | collective-permute-done | bytes 163872 | tf_op jit(solution)/shard_map/ppermute | solution.py:14
  79.1 16.6 %all_to_all.36 = bf16[8,320,128]{2,1,0:T(8,128)(2,1)S(1)} all-to-all(bf16[8,320,128]{2,1,0:T(8,128)(2,1)S(1)} %stack.9), channel_id=1, replica_groups=mesh['section'=8,'eg'=4,'q'=8,'dp'=2] {'q'}, dimensions={0} | all-to-all | bytes 1310720 | tf_op jit(solution)/shard_map/all_to_all | solution.py:67
  95.7 1.7 fusion
  97.7 1.4 reshape.139
  99.1 6.6 %all-to-all-start.3 = ((bf16[64,2,1120]{2,1,0:T(2,128)(2,1)}), bf16[64,2,1120]{2,1,0:T(2,128)(2,1)S(1)}, u32[]{:S(2)}, u32[]{:S(2)}) async-start(bf16[64,2,1120]{2,1,0:T(2,128)(2,1)} %reshape.139), calls=%async_computation.3 | async-start | bytes 589824 | tf_op jit(solution)/shard_map/all_to_all | solution.py:74
  105.9 13.8 %all-to-all-done.3 = bf16[64,2,1120]{2,1,0:T(2,128)(2,1)S(1)} async-done(((bf16[64,2,1120]{2,1,0:T(2,128)(2,1)}), bf16[64,2,1120]{2,1,0:T(2,128)(2,1)S(1)}, u32[]{:S(2)}, u32[]{:S(2)}) %all-to-all-start.3) | async-done | bytes 286752 | tf_op jit(solution)/shard_map/all_to_all | solution.py:74
  122.7 3.1 %collective-permute-start.1 = (bf16[8,7168]{1,0:T(8,128)(2,1)S(1)}, bf16[8,7168]{1,0:T(8,128)(2,1)S(1)}, u32[]{:S(2)}, u32[]{:S(2)}) collective-permute-start(bf16[8,7168]{1,0:T(8,128)(2,1)S(1)} %fusion.17), channel_id=1, source_target_pairs={{0,64},{64,128},{128,192},{192,256},{256,320},{320,384},{384,448},... | collective-permute-start | bytes 344072 | tf_op jit(solution)/shard_map/ppermute | solution.py:14
  125.9 4.7 %collective-permute-done.1 = bf16[8,7168]{1,0:T(8,128)(2,1)S(1)} collective-permute-done((bf16[8,7168]{1,0:T(8,128)(2,1)S(1)}, bf16[8,7168]{1,0:T(8,128)(2,1)S(1)}, u32[]{:S(2)}, u32[]{:S(2)}) %collective-permute-start.1) | collective-permute-done | bytes 114720 | tf_op jit(solution)/shard_map/ppermute | solution.py:14
  131.5 12.6 %all_to_all.37 = bf16[8,2,8960]{2,1,0:T(2,128)(2,1)S(1)} all-to-all(bf16[8,2,8960]{2,1,0:T(2,128)(2,1)S(1)} %reshape.142), channel_id=1, replica_groups=mesh['section'=8,'eg'=4,'q'=8,'dp'=2] {'eg','dp'}, dimensions={0} | all-to-all | bytes 573440 | tf_op jit(solution)/shard_map/all_to_all | solution.py:55
  144.3 0.8 copy.63
  145.1 30.4 %all-gather.5.cloned.1.call-done = bf16[5,64,3584]{2,1,0:T(8,128)(2,1)} async-done(((bf16[5,8,3584]{2,1,0:T(8,128)(2,1)}), bf16[5,64,3584]{2,1,0:T(8,128)(2,1)}) %all-gather.5.cloned.1.call-update) | async-done | bytes 2293776 | tf_op jit(solution)/shard_map/all_gather | solution.py:57
  175.5 2.4 %fusion.36 = (bf16[2,320,128]{2,1,0:T(8,128)(2,1)S(1)}, f32[2,320,128]{2,1,0:T(8,128)S(1)}) fusion(bf16[320,3584,1]{1,0,2:T(8,128)(2,1)} %bitcast.99, bf16[2,128,3584]{2,1,0:T(8,128)(2,1)S(1)} %bitcast.89), kind=kOutput, calls=%fused_computation.78 | convolution fusion | flops 587284480 | bytes 4620288 | tf_op jit(solution)/shard_map/dot_general | solution.py:62
  177.9 2.2 collective-permute-start.2
  180.1 5.1 %collective-permute-done.2 = bf16[2,320,128]{2,1,0:T(8,128)(2,1)S(1)} collective-permute-done((bf16[2,320,128]{2,1,0:T(8,128)(2,1)S(1)}, bf16[2,320,128]{2,1,0:T(8,128)(2,1)S(1)}, u32[]{:S(2)}, u32[]{:S(2)}) %collective-permute-start.2) | collective-permute-done | bytes 163872 | tf_op jit(solution)/shard_map/ppermute | solution.py:14
  185.5 15.9 %all_to_all.38 = bf16[8,320,128]{2,1,0:T(8,128)(2,1)S(1)} all-to-all(bf16[8,320,128]{2,1,0:T(8,128)(2,1)S(1)} %stack.11), channel_id=1, replica_groups=mesh['section'=8,'eg'=4,'q'=8,'dp'=2] {'q'}, dimensions={0} | all-to-all | bytes 1310720 | tf_op jit(solution)/shard_map/all_to_all | solution.py:67
  201.4 1.7 fusion.1
  203.5 1.4 reshape.147
  204.8 9.1 %all-to-all-start.6 = ((bf16[64,2,1120]{2,1,0:T(2,128)(2,1)}), bf16[64,2,1120]{2,1,0:T(2,128)(2,1)S(1)}, u32[]{:S(2)}, u32[]{:S(2)}) async-start(bf16[64,2,1120]{2,1,0:T(2,128)(2,1)} %reshape.147), calls=%async_computation.6 | async-start | bytes 589824 | tf_op jit(solution)/shard_map/all_to_all | solution.py:74
  214.0 13.8 %all-to-all-done.6 = bf16[64,2,1120]{2,1,0:T(2,128)(2,1)S(1)} async-done(((bf16[64,2,1120]{2,1,0:T(2,128)(2,1)}), bf16[64,2,1120]{2,1,0:T(2,128)(2,1)S(1)}, u32[]{:S(2)}, u32[]{:S(2)}) %all-to-all-start.6) | async-done | bytes 286752 | tf_op jit(solution)/shard_map/all_to_all | solution.py:74
  229.1 0.7 gather_fusion.1
  (73 shorter events, 9.9 us)
Async XLA Ops:
  6.5 62.0 %all-gather.3.cloned.1.call-start = ((), (), s32[]{:S(2)}) async-start(), calls=%async_computation.7 | async-start | bytes 2580480 | tf_op jit(solution)/shard_map/all_gather | solution.py:57
  11.6 31.2 %copy-start.2 = (bf16[1,3584,128]{2,1,0:T(8,128)(2,1)S(1)}, bf16[1,3584,128]{2,1,0:T(8,128)(2,1)}, u32[]{:S(2)}) copy-start(bf16[1,3584,128]{2,1,0:T(8,128)(2,1)} %param.12) | copy-start | bytes 2752516
  34.6 44.4 %all-to-all-start.2 = ((bf16[8,448,128]{2,1,0:T(8,128)(2,1)}), bf16[8,448,128]{2,1,0:T(8,128)(2,1)}, u32[]{:S(2)}, u32[]{:S(2)}) async-start(bf16[8,448,128]{2,1,0:T(8,128)(2,1)} %bitcast.16), calls=%async_computation.2 | async-start | bytes 1835008 | tf_op jit(solution)/shard_map/all_to_all | solution.py:92
  71.5 7.4 %collective-permute-start = (bf16[2,320,128]{2,1,0:T(8,128)(2,1)S(1)}, bf16[2,320,128]{2,1,0:T(8,128)(2,1)S(1)}, u32[]{:S(2)}, u32[]{:S(2)}) collective-permute-start(bf16[2,320,128]{2,1,0:T(8,128)(2,1)S(1)} %get-tuple-element.16), channel_id=1, source_target_pairs={{0,1},{1,0},{2,3},{3,2},{4,5},{5,4},{6,7},{7,6},{8,9},{9,8},{10,11... | collective-permute-start | bytes 491528 | tf_op jit(solution)/shard_map/ppermute | solution.py:14
  95.7 10.2 %copy-start.4 = (f32[1,2,8,2]{2,3,1,0:T(2,128)S(1)}, f32[1,2,8,2]{2,3,1,0:T(2,128)}, u32[]{:S(2)}) copy-start(f32[1,2,8,2]{2,3,1,0:T(2,128)} %param.15) | copy-start | bytes 388
  99.1 20.6 %all-to-all-start.3 = ((bf16[64,2,1120]{2,1,0:T(2,128)(2,1)}), bf16[64,2,1120]{2,1,0:T(2,128)(2,1)S(1)}, u32[]{:S(2)}, u32[]{:S(2)}) async-start(bf16[64,2,1120]{2,1,0:T(2,128)(2,1)} %reshape.139), calls=%async_computation.3 | async-start | bytes 589824 | tf_op jit(solution)/shard_map/all_to_all | solution.py:74
  105.8 69.7 %all-gather.5.cloned.1.call-start = ((), (), s32[]{:S(2)}) async-start(), calls=%async_computation.8 | async-start | bytes 2580480 | tf_op jit(solution)/shard_map/all_gather | solution.py:57
  120.9 1.7 copy-start.1
  120.9 9.8 %copy-start.3 = (f32[1,7168]{1,0:T(1,128)S(1)}, f32[1,7168]{1,0:T(1,128)}, u32[]{:S(2)}) copy-start(f32[1,7168]{1,0:T(1,128)} %param.10) | copy-start | bytes 86020
  122.7 7.9 %collective-permute-start.1 = (bf16[8,7168]{1,0:T(8,128)(2,1)S(1)}, bf16[8,7168]{1,0:T(8,128)(2,1)S(1)}, u32[]{:S(2)}, u32[]{:S(2)}) collective-permute-start(bf16[8,7168]{1,0:T(8,128)(2,1)S(1)} %fusion.17), channel_id=1, source_target_pairs={{0,64},{64,128},{128,192},{192,256},{256,320},{320,384},{384,448},... | collective-permute-start | bytes 344072 | tf_op jit(solution)/shard_map/ppermute | solution.py:14
  130.8 44.7 %copy-start = (bf16[256,3584]{1,0:T(8,128)(2,1)S(1)}, bf16[256,3584]{1,0:T(8,128)(2,1)}, u32[]{:S(2)}) copy-start(bf16[256,3584]{1,0:T(8,128)(2,1)} %copy.56) | copy-start | bytes 5505028
  177.9 7.4 %collective-permute-start.2 = (bf16[2,320,128]{2,1,0:T(8,128)(2,1)S(1)}, bf16[2,320,128]{2,1,0:T(8,128)(2,1)S(1)}, u32[]{:S(2)}, u32[]{:S(2)}) collective-permute-start(bf16[2,320,128]{2,1,0:T(8,128)(2,1)S(1)} %get-tuple-element.18), channel_id=1, source_target_pairs={{0,1},{1,0},{2,3},{3,2},{4,5},{5,4},{6,7},{7,6},{8,9},{9,8},{10,11... | collective-permute-start | bytes 491528 | tf_op jit(solution)/shard_map/ppermute | solution.py:14
  204.8 23.0 %all-to-all-start.6 = ((bf16[64,2,1120]{2,1,0:T(2,128)(2,1)}), bf16[64,2,1120]{2,1,0:T(2,128)(2,1)S(1)}, u32[]{:S(2)}, u32[]{:S(2)}) async-start(bf16[64,2,1120]{2,1,0:T(2,128)(2,1)} %reshape.147), calls=%async_computation.6 | async-start | bytes 589824 | tf_op jit(solution)/shard_map/all_to_all | solution.py:74
Sparse Core Ops, SparseCore 0:
  34.8 33.7 all-gather.2
  145.2 30.2 all-gather.4
